TPU v7x, 32 devices: a whole 2x2x4 slice. The times are simulated.
32 devices in a mesh: ctx: 4 (over y, x), tp: 8 (over z, core).
Axes of the slice: x: 2, y: 2, z: 4, core: 2. Of those that a mesh axis runs over, the one named last changes fastest.
Arguments:
- resid: bfloat16 [1024, 4096], P('ctx', 'tp'), may hold values from -6 to 6
- attn_gain: bfloat16 [4096], replicated, may hold values from 0.5 to 1.5
- mlp_gain: bfloat16 [4096], replicated, may hold values from 0.5 to 1.5
- w_query: bfloat16 [4096, 4096], P(None, 'tp'), may hold values from -0.09375 to 0.09375
- w_kv: bfloat16 [4096, 1024], P(None, 'tp'), may hold values from -0.09375 to 0.09375
- w_out: bfloat16 [4096, 4096], P('tp'), may hold values from -0.09375 to 0.09375
- w_gate: bfloat16 [4096, 11008], P(None, 'tp'), may hold values from -0.09375 to 0.09375
- w_up: bfloat16 [4096, 11008], P(None, 'tp'), may hold values from -0.09375 to 0.09375
- w_down: bfloat16 [11008, 4096], P('tp'), may hold values from -0.0546875 to 0.0546875
- kv_cache: bfloat16 [32, 128, 1024], P('ctx'), may hold values from -70 to 70
- cache_len: int32 [4], replicated, may hold values from 1 to 2048
- span_len: int32 [4], replicated, may hold values from 1 to 256
- slot_req: int32 [32], P('ctx'), may hold values from 0 to 4, as said below
- slot_blk: int32 [32], P('ctx'), may hold values from 0 to 15, as said below
Outputs:
- layer_out: bfloat16 [1024, 4096], P('ctx', 'tp')
- new_kv: bfloat16 [1024, 1024], P('ctx', 'tp')
Inputs may be any that keep to these rules, and one draw needn't show every extreme that they name: `slot_req`: each request r holds ceil(cache_len[r] / 128) blocks, and each of its blocks stands in exactly one slot; every other slot is empty. `slot_blk`: block numbers of live slots are below their request's block count; empty slots carry 0.
All inputs are finite; a program needn't handle non-finite values.
Results may differ from a plain program's by a relative error of at most 0.035.
Values may be sent and summed in bfloat16 or wider, within the bound.
No kernel may reach another device: no remote copies, remote signals or barrier semaphores. Data moves between devices by JAX's collectives and lax.ppermute only.
A program may use at most 128 MiB of HBM per device.

v0:
```python
import jax
import jax.numpy as jnp
from jax import lax
from jax.sharding import PartitionSpec as P

HQ = 32
KVH = 4
HD = 128
BLK = 128
THETA = 5000000.0
EPS = 1e-05
NEG = -1e30


def rms_norm(values, gain):
    wide = values.astype(jnp.float32)
    factor = lax.rsqrt(jnp.mean(wide * wide, axis=-1, keepdims=True) + EPS)
    return (wide * factor * gain.astype(jnp.float32)).astype(jnp.bfloat16)


def rotate(vectors, positions):
    width = vectors.shape[-1]
    half = width // 2
    freqs = THETA ** (-(jnp.arange(half, dtype=jnp.float32) * 2.0 / width))
    angles = positions.astype(jnp.float32)[:, None] * freqs[None, :]
    cosine = jnp.cos(angles)[:, None, :]
    sine = jnp.sin(angles)[:, None, :]
    first = vectors[..., :half]
    second = vectors[..., half:]
    return jnp.concatenate(
        [first * cosine - second * sine, second * cosine + first * sine], axis=-1
    )


def column_term(rows, weight):
    return lax.dot_general(
        weight, rows, (((0,), (1,)), ((), ())), preferred_element_type=jnp.float32
    )


def gather_ctx(value, count):
    parts = [value]
    for shift in range(1, count):
        pairs = [(i, (i + shift) % count) for i in range(count)]
        parts.append(lax.ppermute(value, "ctx", pairs))
    return parts


def per_device(
    resid,
    attn_gain,
    mlp_gain,
    w_query,
    w_kv,
    w_out,
    w_gate,
    w_up,
    w_down,
    kv_cache,
    cache_len,
    span_len,
    slot_req,
    slot_blk,
):
    span_size = resid.shape[0]
    ctx_count = lax.axis_size("ctx")
    q_cols = w_query.shape[1]
    heads_dev = q_cols // HD
    ctx_rank = lax.axis_index("ctx")
    tp_rank = lax.axis_index("tp")
    group = tp_rank * heads_dev // (HQ // KVH)
    my_len = cache_len[ctx_rank]
    my_span = span_len[ctx_rank]
    offsets = jnp.arange(span_size, dtype=jnp.int32)
    positions = my_len + offsets
    live_rows = offsets < my_span
    own_cache = jnp.concatenate(
        [
            lax.dynamic_slice_in_dim(kv_cache, group * HD, HD, 2),
            lax.dynamic_slice_in_dim(kv_cache, KVH * HD + group * HD, HD, 2),
        ],
        axis=2,
    )
    own_meta = jnp.stack([slot_req, slot_blk])
    cache_all = jnp.concatenate(gather_ctx(own_cache, ctx_count), axis=0)
    meta_all = jnp.concatenate(gather_ctx(own_meta, ctx_count), axis=1)
    full_resid = lax.all_gather(resid, "tp", axis=1, tiled=True)
    x_norm = rms_norm(full_resid, attn_gain)
    query = rotate(
        jnp.dot(x_norm, w_query, preferred_element_type=jnp.float32).reshape(
            span_size, heads_dev, HD
        ),
        positions,
    ).astype(jnp.bfloat16)
    kv_piece = jnp.dot(x_norm, w_kv, preferred_element_type=jnp.float32).astype(jnp.bfloat16)
    kv_width = kv_piece.shape[1]
    kv_all = lax.all_gather(kv_piece, "tp", axis=1, tiled=True)
    all_keys = rotate(
        kv_all[:, : KVH * HD].astype(jnp.float32).reshape(span_size, KVH, HD), positions
    ).astype(jnp.bfloat16)
    joined = jnp.concatenate([all_keys.reshape(span_size, KVH * HD), kv_all[:, KVH * HD :]], axis=1)
    mine = lax.dynamic_slice_in_dim(joined, tp_rank * kv_width, kv_width, 1)
    new_kv = jnp.where(live_rows[:, None], mine, jnp.zeros_like(mine))
    new_keys = lax.dynamic_index_in_dim(all_keys, group, 1, keepdims=False)
    new_vals = lax.dynamic_slice_in_dim(kv_all, KVH * HD + group * HD, HD, 1)
    cache_rows = cache_all.shape[0] * BLK
    keys = jnp.concatenate([cache_all[..., :HD].reshape(cache_rows, HD), new_keys], axis=0)
    vals = jnp.concatenate([cache_all[..., HD:].reshape(cache_rows, HD), new_vals], axis=0)
    key_pos = meta_all[1][:, None] * BLK + jnp.arange(BLK, dtype=jnp.int32)[None, :]
    cache_ok = ((meta_all[0][:, None] == ctx_rank) & (key_pos < my_len)).reshape(cache_rows)
    new_ok = (offsets[None, :] <= offsets[:, None]) & (offsets[None, :] < my_span)
    valid = jnp.concatenate(
        [jnp.broadcast_to(cache_ok[None, :], (span_size, cache_rows)), new_ok], axis=1
    )
    scores = jnp.einsum("chd,kd->hck", query, keys, preferred_element_type=jnp.float32) * HD ** (
        -0.5
    )
    peak = jnp.max(jnp.where(valid[None], scores, NEG), axis=2)
    weights = jnp.where(valid[None], jnp.exp(scores - peak[..., None]), 0.0)
    total = jnp.sum(weights, axis=2)
    summed = jnp.einsum(
        "hck,kd->hcd", weights.astype(jnp.bfloat16), vals, preferred_element_type=jnp.float32
    )
    attn_rows = (
        (summed / total[..., None])
        .transpose(1, 0, 2)
        .reshape(span_size, q_cols)
        .astype(jnp.bfloat16)
    )
    head_sum = lax.psum(
        jnp.dot(attn_rows, w_out, preferred_element_type=jnp.float32).astype(jnp.bfloat16), "tp"
    )
    full_mid = (full_resid.astype(jnp.float32) + head_sum.astype(jnp.float32)).astype(jnp.bfloat16)
    mid = lax.dynamic_slice_in_dim(full_mid, tp_rank * resid.shape[1], resid.shape[1], 1)
    x_two = rms_norm(full_mid, mlp_gain)
    gate = jnp.dot(x_two, w_gate, preferred_element_type=jnp.float32)
    up_part = jnp.dot(x_two, w_up, preferred_element_type=jnp.float32)
    hidden = (jax.nn.silu(gate) * up_part).astype(jnp.bfloat16)
    down_sum = lax.psum_scatter(
        column_term(hidden, w_down).astype(jnp.bfloat16), "tp", scatter_dimension=0, tiled=True
    ).astype(jnp.float32)
    layer_out = (mid.astype(jnp.float32) + down_sum.T).astype(jnp.bfloat16)
    layer_out = jnp.where(live_rows[:, None], layer_out, jnp.zeros_like(layer_out))
    return (layer_out, new_kv)


def solution(mesh):
    return jax.shard_map(
        per_device,
        mesh=mesh,
        in_specs=(
            P("ctx", "tp"),
            P(),
            P(),
            P(None, "tp"),
            P(None, "tp"),
            P("tp", None),
            P(None, "tp"),
            P(None, "tp"),
            P("tp", None),
            P("ctx", None, None),
            P(),
            P(),
            P("ctx"),
            P("ctx"),
        ),
        out_specs=(P("ctx", "tp"), P("ctx", "tp")),
        check_vma=False,
    )
```

profile of v0, /device:TPU:0, one launch (start us, length us, event | category | flops | bytes accessed | tf_op | source)
XLA Modules:
  0.0 248.4 jit_solution(2127436485068741131)
XLA Ops:
  8.6 3.9 %collective-permute-start.2 = (s32[2,8]{1,0:T(2,128)S(1)}, s32[2,8]{1,0:T(2,128)S(1)}, u32[]{:S(2)}, u32[]{:S(2)}) collective-permute-start(s32[2,8]{1,0:T(2,128)S(1)} %pad_add_fusion.1), channel_id=1, source_target_pairs={{0,24},{8,0},{16,8},{24,16},{1,25},{9,1},{17,9},{25,17},{2,26},{10... | collective-permute-start | bytes 200 | tf_op jit(solution)/shard_map/ppermute | solution.py:45
  13.6 1.1 constant_dynamic-slice_fusion.2
  14.8 2.4 collective-permute-start.5
  17.2 1.5 collective-permute-start.4
  18.7 1.2 dynamic_slice.25
  19.9 1.3 dynamic_slice.26
  23.3 1.2 multiply_cosine_fusion
  24.5 0.8 pad_add_fusion.2
  26.0 5.1 %pad_add_fusion = pred[256,4352]{0,1:T(8,128)(4,1)} fusion(pred[256,256]{0,1:T(8,128)(4,1)S(1)} %fusion.45, pred[4352]{0:T(1024)(128)(4,1)S(1)} %pad.8.clone), kind=kLoop, calls=%fused_computation.20 | loop fusion | flops 1114112 | bytes 1184000 | tf_op jit(solution)/shard_map/concatenate | solution.py:112
  31.1 9.8 %collective-permute-done.4 = bf16[8,128,256]{2,1,0:T(8,128)(2,1)S(1)} collective-permute-done((bf16[8,128,256]{2,1,0:T(8,128)(2,1)S(1)}, bf16[8,128,256]{2,1,0:T(8,128)(2,1)S(1)}, u32[]{:S(2)}, u32[]{:S(2)}) %collective-permute-start.4) | collective-permute-done | bytes 524320 | tf_op jit(solution)/shard_map/ppermute | solution.py:45
  41.2 1.6 fusion.56
  42.8 1.3 copy.25
  44.1 2.2 fusion.14
  46.3 2.4 convolution_convert_fusion.2
  48.7 14.3 %all_gather.7 = bf16[256,1024]{1,0:T(8,128)(2,1)S(1)} all-gather(bf16[256,128]{1,0:T(8,128)(2,1)S(1)} %convolution_convert_fusion.2), channel_id=1, replica_groups=mesh['ctx'=4,'tp'=8] {'tp'}, dimensions={1}, use_global_device_ids=true | all-gather | bytes 589824 | tf_op jit(solution)/shard_map/all_gather | solution.py:97
  63.0 0.9 fusion.57
  63.9 0.7 copy.21
  64.7 3.5 %fusion.37 = f32[256,512]{1,0:T(8,128)S(1)} fusion(bf16[4096,512]{1,0:T(8,128)(2,1)} %param.17, bf16[256,4096]{1,0:T(8,128)(2,1)S(1)} %copy-done.2, f32[4096]{0:T(1024)S(1)} %convert_element_type.74, f32[256]{0:T(256)S(1)} %add_rsqrt_fusion.1), kind=kOutput, calls=%fused_computation.43 | convolution fusion | flops 1077936128 | bytes 6833152 | tf_op jit(solution)/shard_map/dot_general | solution.py:90
  68.4 1.2 reshape.161
  70.3 1.0 multiply_subtract_fusion
  71.5 1.0 subtract_convert_fusion
  72.6 8.7 %fusion.30 = f32[4352,256,4]{1,0,2:T(8,128)} fusion(bf16[256,128]{1,0:T(8,128)(2,1)S(1)} %dynamic-slice_bitcast_fusion, bf16[4096,128]{1,0:T(8,128)(2,1)S(1)} %bitcast.63, bf16[256,4,64]{2,0,1:T(8,128)(2,1)S(1)} %get-tuple-element.9, bf16[256,4,64]{2,0,1:T(8,128)(2,1)S(1)} %get-tuple-element.8), kind=kOutput, calls=%fused_computation.39 | convolution fusion | flops 1143603200 | bytes 19202048 | tf_op jit(solution)/shard_map/chd,kd->hck/dot_general | solution.py:115
  81.2 18.7 %fusion.60 = (f32[4,256]{1,0:T(4,128)S(1)}, bf16[4,256,4352]{1,2,0:T(8,128)(2,1)}) fusion(f32[4352,256,4]{1,0,2:T(8,128)} %fusion.30, pred[256,4352]{0,1:T(8,128)(4,1)} %pad_add_fusion), kind=kOutput, calls=%fused_computation.91 | output fusion | flops 31199488 | bytes 27856896 | tf_op jit(solution)/shard_map/sub | solution.py:119
  100.0 5.3 %fusion.25 = bf16[256,4,128]{0,2,1:T(8,128)(2,1)S(1)} fusion(bf16[4,256,4352]{1,2,0:T(8,128)(2,1)} %get-tuple-element.21, bf16[256,128]{0,1:T(8,128)(2,1)S(1)} %copy-done.8, bf16[4096,128]{0,1:T(8,128)(2,1)} %copy.25, f32[256,4]{0,1:T(4,128)S(1)} %bitcast.70), kind=kOutput, calls=%fused_computation.33 | convolution fusion | flops 1143341056 | bytes 10293248 | tf_op jit(solution)/shard_map/hck,kd->hcd/dot_general | solution.py:121
  105.3 2.7 %convolution_convert_fusion = bf16[256,4096]{1,0:T(8,128)(2,1)} fusion(bf16[256,512]{0,1:T(8,128)(2,1)S(1)} %bitcast.65, bf16[512,4096]{1,0:T(8,128)(2,1)S(1)} %copy-done.3), kind=kOutput, calls=%fused_computation.17 | convolution fusion | flops 1074790400 | bytes 6553600 | tf_op jit(solution)/shard_map/dot_general | solution.py:131
  108.1 63.7 %all-reduce.2.cloned.1.call-done = bf16[256,4096]{1,0:T(8,128)(2,1)} async-done(((bf16[256,4096]{1,0:T(8,128)(2,1)}), bf16[256,4096]{1,0:T(8,128)(2,1)}) %all-reduce.2.cloned.1.call-update) | async-done | bytes 2097168 | tf_op jit(solution)/shard_map/psum | solution.py:130
  171.8 3.9 %fusion.11 = (f32[256]{0:T(256)S(1)}, bf16[256,4096]{1,0:T(8,128)(2,1)}) fusion(bf16[256,4096]{1,0:T(8,128)(2,1)} %all-reduce.2.cloned.1.call-done, bf16[256,4096]{1,0:T(8,128)(2,1)S(1)} %copy-done.2), kind=kLoop, calls=%fused_computation.21 | loop fusion | flops 7339776 | bytes 6292480 | tf_op jit(solution)/shard_map/reduce_sum | solution.py:17
  175.7 7.0 %fusion.35 = f32[256,1376]{0,1:T(8,128)S(1)} fusion(bf16[4096,1376]{0,1:T(8,128)(2,1)} %param.20, bf16[256,4096]{1,0:T(8,128)(2,1)} %get-tuple-element.3, f32[4096]{0:T(1024)S(1)} %convert_element_type.87, f32[256]{0:T(256)S(1)} %add_rsqrt_fusion), kind=kOutput, calls=%fused_computation.42 | convolution fusion | flops 2889875456 | bytes 14795776 | tf_op jit(solution)/shard_map/dot_general | solution.py:136
  182.7 21.7 %fusion.10 = bf16[4096,256]{0,1:T(8,128)(2,1)} fusion(bf16[1376,4096]{1,0:T(8,128)(2,1)} %param.22, bf16[4096,1376]{0,1:T(8,128)(2,1)} %param.21, f32[256,1376]{0,1:T(8,128)S(1)} %fusion.35, bf16[256,4096]{1,0:T(8,128)(2,1)} %get-tuple-element.3, f32[4096]{0:T(1024)S(1)} %convert_element_type.87, f32[256]{0:T(256)S(1)} %add_rsqrt_fusion), kind=kOutput, calls=%fused_computation.19 | convolution fusion | flops 5778718720 | bytes 28165120 | tf_op jit(solution)/shard_map/dot_general | solution.py:36
  204.6 0.7 fusion.47
  205.4 34.7 %reduce-scatter.2.cloned.1.call-done = bf16[512,256]{0,1:T(8,128)(2,1)} async-done(((bf16[4096,256]{0,1:T(8,128)(2,1)}), bf16[512,256]{0,1:T(8,128)(2,1)}) %reduce-scatter.2.cloned.1.call-update) | async-done | bytes 262160 | tf_op jit(solution)/shard_map/reduce_scatter | solution.py:139
  240.1 1.8 fusion.41
  (57 shorter events, 7.1 us)
Async XLA Ops:
  7.2 39.1 %copy-start = (bf16[4096,128]{1,0:T(8,128)(2,1)S(1)}, bf16[4096,128]{1,0:T(8,128)(2,1)}, u32[]{:S(2)}) copy-start(bf16[4096,128]{1,0:T(8,128)(2,1)} %param.18) | copy-start | bytes 3145732
  7.2 36.9 %all-gather.2.cloned.1.call-start = ((), (), s32[]{:S(2)}) async-start(), calls=%async_computation.1 | async-start | bytes 2359296 | tf_op jit(solution)/shard_map/all_gather | solution.py:87
  7.9 163.9 %all-reduce.2.cloned.1.call-start = ((), (), s32[]{:S(2)}) async-start(), calls=%async_computation.2 | async-start | bytes 4194304 | tf_op jit(solution)/shard_map/psum | solution.py:130
  8.6 15.9 %collective-permute-start.2 = (s32[2,8]{1,0:T(2,128)S(1)}, s32[2,8]{1,0:T(2,128)S(1)}, u32[]{:S(2)}, u32[]{:S(2)}) collective-permute-start(s32[2,8]{1,0:T(2,128)S(1)} %pad_add_fusion.1), channel_id=1, source_target_pairs={{0,24},{8,0},{16,8},{24,16},{1,25},{9,1},{17,9},{25,17},{2,26},{10... | collective-permute-start | bytes 200 | tf_op jit(solution)/shard_map/ppermute | solution.py:45
  12.5 12.0 %collective-permute-start.1 = (s32[2,8]{1,0:T(2,128)S(1)}, s32[2,8]{1,0:T(2,128)S(1)}, u32[]{:S(2)}, u32[]{:S(2)}) collective-permute-start(s32[2,8]{1,0:T(2,128)S(1)} %pad_add_fusion.1), channel_id=1, source_target_pairs={{0,16},{8,24},{16,0},{24,8},{1,17},{9,25},{17,1},{25,9},{2,18},{10... | collective-permute-start | bytes 200 | tf_op jit(solution)/shard_map/ppermute | solution.py:45
  13.0 11.5 %collective-permute-start = (s32[2,8]{1,0:T(2,128)S(1)}, s32[2,8]{1,0:T(2,128)S(1)}, u32[]{:S(2)}, u32[]{:S(2)}) collective-permute-start(s32[2,8]{1,0:T(2,128)S(1)} %pad_add_fusion.1), channel_id=1, source_target_pairs={{0,8},{8,16},{16,24},{24,0},{1,9},{9,17},{17,25},{25,1},{2,10},{10... | collective-permute-start | bytes 200 | tf_op jit(solution)/shard_map/ppermute | solution.py:45
  14.8 16.4 %collective-permute-start.5 = (bf16[8,128,256]{2,1,0:T(8,128)(2,1)S(1)}, bf16[8,128,256]{2,1,0:T(8,128)(2,1)S(1)}, u32[]{:S(2)}, u32[]{:S(2)}) collective-permute-start(bf16[8,128,256]{2,1,0:T(8,128)(2,1)S(1)} %pad_maximum_fusion.1), channel_id=1, source_target_pairs={{0,24},{8,0},{16,8},{24,16},{1,25},{9,1},{17,9},{25,17},{2,26},{10... | collective-permute-start | bytes 1572872 | tf_op jit(solution)/shard_map/ppermute | solution.py:45
  17.2 23.8 %collective-permute-start.4 = (bf16[8,128,256]{2,1,0:T(8,128)(2,1)S(1)}, bf16[8,128,256]{2,1,0:T(8,128)(2,1)S(1)}, u32[]{:S(2)}, u32[]{:S(2)}) collective-permute-start(bf16[8,128,256]{2,1,0:T(8,128)(2,1)S(1)} %pad_maximum_fusion.1), channel_id=1, source_target_pairs={{0,16},{8,24},{16,0},{24,8},{1,17},{9,25},{17,1},{25,9},{2,18},{10... | collective-permute-start | bytes 1572872 | tf_op jit(solution)/shard_map/ppermute | solution.py:45
  24.5 16.4 %collective-permute-start.3 = (bf16[8,128,256]{2,1,0:T(8,128)(2,1)S(1)}, bf16[8,128,256]{2,1,0:T(8,128)(2,1)S(1)}, u32[]{:S(2)}, u32[]{:S(2)}) collective-permute-start(bf16[8,128,256]{2,1,0:T(8,128)(2,1)S(1)} %pad_maximum_fusion.1), channel_id=1, source_target_pairs={{0,8},{8,16},{16,24},{24,0},{1,9},{9,17},{17,25},{25,1},{2,10},{10... | collective-permute-start | bytes 1572872 | tf_op jit(solution)/shard_map/ppermute | solution.py:45
  44.1 20.6 %copy-start.2 = (bf16[256,4096]{1,0:T(8,128)(2,1)S(1)}, bf16[256,4096]{1,0:T(8,128)(2,1)}, u32[]{:S(2)}) copy-start(bf16[256,4096]{1,0:T(8,128)(2,1)} %all-gather.2.cloned.1.call-done) | copy-start | bytes 6291460
  69.6 3.0 %copy-start.4 = (bf16[32,128,128]{2,1,0:T(8,128)(2,1)S(1)}, bf16[32,128,128]{2,1,0:T(8,128)(2,1)}, u32[]{:S(2)}) copy-start(bf16[32,128,128]{2,1,0:T(8,128)(2,1)} %get-tuple-element.5) | copy-start | bytes 3145732
  71.3 9.9 %copy-start.5 = (bf16[256,4,64]{2,0,1:T(8,128)(2,1)}, bf16[256,4,64]{2,0,1:T(8,128)(2,1)S(1)}, u32[]{:S(2)}) copy-start(bf16[256,4,64]{2,0,1:T(8,128)(2,1)S(1)} %get-tuple-element.11) | copy-start | bytes 393220
  81.2 18.7 %copy-start.8 = (bf16[256,128]{0,1:T(8,128)(2,1)S(1)}, bf16[256,128]{0,1:T(8,128)(2,1)}, u32[]{:S(2)}) copy-start(bf16[256,128]{0,1:T(8,128)(2,1)} %copy.21) | copy-start | bytes 196612
  100.0 5.3 %copy-start.3 = (bf16[512,4096]{1,0:T(8,128)(2,1)S(1)}, bf16[512,4096]{1,0:T(8,128)(2,1)}, u32[]{:S(2)}) copy-start(bf16[512,4096]{1,0:T(8,128)(2,1)} %param.19) | copy-start | bytes 12582916
  105.3 2.7 %copy-start.9 = (bf16[4096]{0:T(1024)(128)(2,1)S(1)}, bf16[4096]{0:T(1024)(128)(2,1)}, u32[]{:S(2)}) copy-start(bf16[4096]{0:T(1024)(128)(2,1)} %param.16) | copy-start | bytes 24580
  108.0 132.1 %reduce-scatter.2.cloned.1.call-start = ((), (), s32[]{:S(2)}) async-start(), calls=%async_computation.3 | async-start | bytes 2359296 | tf_op jit(solution)/shard_map/reduce_scatter | solution.py:139
  182.7 21.8 %copy-start.6 = (bf16[256,4,64]{2,0,1:T(8,128)(2,1)S(1)}, bf16[256,4,64]{2,0,1:T(8,128)(2,1)}, u32[]{:S(2)}) copy-start(bf16[256,4,64]{2,0,1:T(8,128)(2,1)} %copy-done.5) | copy-start | bytes 393220
  182.7 21.9 %copy-start.7 = (bf16[256,512]{1,0:T(8,128)(2,1)S(1)}, bf16[256,512]{1,0:T(8,128)(2,1)}, u32[]{:S(2)}) copy-start(bf16[256,512]{1,0:T(8,128)(2,1)} %get-tuple-element.12) | copy-start | bytes 786436
  182.7 59.2 %copy-start.1 = (bf16[4096,128]{1,0:T(8,128)(2,1)S(1)}, bf16[4096,128]{1,0:T(8,128)(2,1)}, u32[]{:S(2)}) copy-start(bf16[4096,128]{1,0:T(8,128)(2,1)} %param.18) | copy-start | bytes 3145732
Sparse Core Ops, SparseCore 0:
  9.6 31.7 all-gather.1
  108.1 63.6 all-reduce.1
  204.6 35.4 reduce-scatter.1
where the time goes:
time: 249 us; the launch traced here: 248 us
  waiting for transfers between devices  109 us (44%)
  matrix products  51.2 us (21%)
  other arithmetic  41.7 us (17%)
  blocking collectives  14.3 us (6%)
  between operations  14 us (6%)
  local copies, waits for them, and re-layouts  9.32 us (4%)
  starting transfers between devices  9.02 us (4%)
    psum x1, waiting for transfers between devices, per_device(): lax.psum(jnp.dot(attn_rows, w_out, preferred_element_type=jnp.float32).as...  63.7 us
    reduce_scatter x1, waiting for transfers between devices, per_device(): lax.psum_scatter(column_term(hidden, w_down).astype(jnp.bfloat16), 'tp',...  34.7 us
    dot_general x1, matrix products, column_term(): lax.dot_general(weight, rows, (((0,), (1,)), ((), ())), preferred_element...  21.7 us
    sub x1, other arithmetic, per_device(): weights = jnp.where(valid[None], jnp.exp(scores - peak[..., None]), 0.0)  18.7 us
    all_gather x1, blocking collectives, per_device(): kv_all = lax.all_gather(kv_piece, 'tp', axis=1, tiled=True)  14.3 us
    ppermute x6, waiting for transfers between devices, gather_ctx(): parts.append(lax.ppermute(value, 'ctx', pairs))  9.82 us
    ppermute x6, starting transfers between devices, gather_ctx(): parts.append(lax.ppermute(value, 'ctx', pairs))  8.9 us
    dot_general x1, matrix products, per_device(): jnp.einsum('chd,kd->hck', query, keys, preferred_element_type=jnp.float32)  8.67 us
  transfers between devices with their start and end apart: 9, of which 3 were waited for; matrix products, arithmetic and copies ran while one was open for 7% of the time, Pallas kernels for 0%

commit v1 on v0

--- a/solution.py
+++ b/solution.py
@@ -127,8 +127,11 @@
         .reshape(span_size, q_cols)
         .astype(jnp.bfloat16)
     )
-    head_sum = lax.psum(
-        jnp.dot(attn_rows, w_out, preferred_element_type=jnp.float32).astype(jnp.bfloat16), "tp"
+    head_sum = jnp.sum(
+        lax.all_gather(
+            jnp.dot(attn_rows, w_out, preferred_element_type=jnp.float32).astype(jnp.bfloat16), "tp"
+        ),
+        axis=0,
     )
     full_mid = (full_resid.astype(jnp.float32) + head_sum.astype(jnp.float32)).astype(jnp.bfloat16)
     mid = lax.dynamic_slice_in_dim(full_mid, tp_rank * resid.shape[1], resid.shape[1], 1)

time: 249 us -> 344 us (1.38)
  waiting for transfers between devices: 109 us -> 194 us
  other arithmetic: 41.7 us -> 50.9 us
    all_gather x0 -> x1, waiting for transfers between devices: none -> 150 us  [per_device(): lax.all_gather(jnp.dot(attn_rows, w_out, preferred_element_type=jnp.float...]
    psum x1 -> x0, waiting for transfers between devices: 63.7 us -> none  [per_device(): lax.psum(jnp.dot(attn_rows, w_out, preferred_element_type=jnp.float32).as...]
    reduce_sum x0 -> x1, other arithmetic: none -> 10.5 us  [per_device(): jnp.sum(lax.all_gather(jnp.dot(attn_rows, w_out, preferred_element_type=j...]
  transfers between devices with their start and end apart: 9 -> 9, of which waited for: 3 -> 3; matrix products, arithmetic and copies ran while one was open for 7% -> 5% of each run, Pallas kernels for 0% -> 0%
where the time goes in v1:
time: 344 us; the launch traced here: 343 us
  waiting for transfers between devices  194 us (56%)
  other arithmetic  50.9 us (15%)
  matrix products  50.6 us (15%)
  blocking collectives  14.3 us (4%)
  between operations  14 us (4%)
  local copies, waits for them, and re-layouts  10.7 us (3%)
  starting transfers between devices  9.02 us (3%)
    all_gather x1, waiting for transfers between devices, per_device(): lax.all_gather(jnp.dot(attn_rows, w_out, preferred_element_type=jnp.float...  150 us
    reduce_scatter x1, waiting for transfers between devices, per_device(): lax.psum_scatter(column_term(hidden, w_down).astype(jnp.bfloat16), 'tp',...  33.3 us
    dot_general x1, matrix products, column_term(): lax.dot_general(weight, rows, (((0,), (1,)), ((), ())), preferred_element...  21.7 us
    sub x1, other arithmetic, per_device(): weights = jnp.where(valid[None], jnp.exp(scores - peak[..., None]), 0.0)  18.8 us
    all_gather x1, blocking collectives, per_device(): kv_all = lax.all_gather(kv_piece, 'tp', axis=1, tiled=True)  14.3 us
    reduce_sum x1, other arithmetic, per_device(): jnp.sum(lax.all_gather(jnp.dot(attn_rows, w_out, preferred_element_type=j...  10.5 us
    ppermute x6, waiting for transfers between devices, gather_ctx(): parts.append(lax.ppermute(value, 'ctx', pairs))  9.8 us
    ppermute x6, starting transfers between devices, gather_ctx(): parts.append(lax.ppermute(value, 'ctx', pairs))  8.9 us
  transfers between devices with their start and end apart: 9, of which 3 were waited for; matrix products, arithmetic and copies ran while one was open for 5% of the time, Pallas kernels for 0%

profile of v1, /device:TPU:0, one launch (start us, length us, event | category | flops | bytes accessed | tf_op | source)
XLA Modules:
  0.0 343.1 jit_solution(17031306400249498253)
XLA Ops:
  8.6 3.9 %collective-permute-start.2 = (s32[2,8]{1,0:T(2,128)S(1)}, s32[2,8]{1,0:T(2,128)S(1)}, u32[]{:S(2)}, u32[]{:S(2)}) collective-permute-start(s32[2,8]{1,0:T(2,128)S(1)} %pad_add_fusion.1), channel_id=1, source_target_pairs={{0,24},{8,0},{16,8},{24,16},{1,25},{9,1},{17,9},{25,17},{2,26},{10... | collective-permute-start | bytes 200 | tf_op jit(solution)/shard_map/ppermute | solution.py:45
  13.6 1.1 constant_dynamic-slice_fusion.2
  14.8 2.4 collective-permute-start.5
  17.2 1.5 collective-permute-start.4
  18.7 1.2 dynamic_slice.25
  19.9 1.3 dynamic_slice.26
  23.3 1.2 multiply_cosine_fusion
  24.5 0.8 pad_add_fusion.2
  26.0 5.1 %pad_add_fusion = pred[256,4352]{0,1:T(8,128)(4,1)} fusion(pred[256,256]{0,1:T(8,128)(4,1)S(1)} %fusion.45, pred[4352]{0:T(1024)(128)(4,1)S(1)} %pad.8.clone), kind=kLoop, calls=%fused_computation.20 | loop fusion | flops 1114112 | bytes 1184000 | tf_op jit(solution)/shard_map/concatenate | solution.py:112
  31.2 9.8 %collective-permute-done.4 = bf16[8,128,256]{2,1,0:T(8,128)(2,1)S(1)} collective-permute-done((bf16[8,128,256]{2,1,0:T(8,128)(2,1)S(1)}, bf16[8,128,256]{2,1,0:T(8,128)(2,1)S(1)}, u32[]{:S(2)}, u32[]{:S(2)}) %collective-permute-start.4) | collective-permute-done | bytes 524320 | tf_op jit(solution)/shard_map/ppermute | solution.py:45
  41.2 1.6 fusion.56
  42.8 1.3 copy.25
  44.1 2.2 fusion.14
  46.4 2.4 convolution_convert_fusion.2
  48.8 14.3 %all_gather.13 = bf16[256,1024]{1,0:T(8,128)(2,1)S(1)} all-gather(bf16[256,128]{1,0:T(8,128)(2,1)S(1)} %convolution_convert_fusion.2), channel_id=1, replica_groups=mesh['ctx'=4,'tp'=8] {'tp'}, dimensions={1}, use_global_device_ids=true | all-gather | bytes 589824 | tf_op jit(solution)/shard_map/all_gather | solution.py:97
  63.1 0.9 fusion.57
  64.7 3.5 %fusion.37 = f32[256,512]{1,0:T(8,128)S(1)} fusion(bf16[4096,512]{1,0:T(8,128)(2,1)} %param.17, bf16[256,4096]{1,0:T(8,128)(2,1)S(1)} %copy-done.2, f32[4096]{0:T(1024)S(1)} %convert_element_type.76, f32[256]{0:T(256)S(1)} %add_rsqrt_fusion.1), kind=kOutput, calls=%fused_computation.43 | convolution fusion | flops 1077936128 | bytes 6833152 | tf_op jit(solution)/shard_map/dot_general | solution.py:90
  68.4 1.2 reshape.161
  70.3 1.0 multiply_subtract_fusion
  71.5 1.0 subtract_convert_fusion
  72.6 8.7 %fusion.30 = f32[4352,256,4]{1,0,2:T(8,128)} fusion(bf16[256,128]{1,0:T(8,128)(2,1)S(1)} %dynamic-slice_bitcast_fusion, bf16[4096,128]{1,0:T(8,128)(2,1)S(1)} %bitcast.65, bf16[256,4,64]{2,0,1:T(8,128)(2,1)S(1)} %get-tuple-element.9, bf16[256,4,64]{2,0,1:T(8,128)(2,1)S(1)} %get-tuple-element.8), kind=kOutput, calls=%fused_computation.39 | convolution fusion | flops 1143603200 | bytes 19202048 | tf_op jit(solution)/shard_map/chd,kd->hck/dot_general | solution.py:115
  81.3 18.8 %fusion.60 = (f32[4,256]{1,0:T(4,128)S(1)}, bf16[4,256,4352]{1,2,0:T(8,128)(2,1)}) fusion(f32[4352,256,4]{1,0,2:T(8,128)} %fusion.30, pred[256,4352]{0,1:T(8,128)(4,1)} %pad_add_fusion), kind=kOutput, calls=%fused_computation.91 | output fusion | flops 31199488 | bytes 27856896 | tf_op jit(solution)/shard_map/sub | solution.py:119
  100.1 5.3 %fusion.25 = bf16[256,4,128]{0,2,1:T(8,128)(2,1)S(1)} fusion(bf16[4,256,4352]{1,2,0:T(8,128)(2,1)} %get-tuple-element.21, bf16[256,128]{0,1:T(8,128)(2,1)S(1)} %copy-done.9, bf16[4096,128]{0,1:T(8,128)(2,1)} %copy.25, f32[256,4]{0,1:T(4,128)S(1)} %bitcast.72), kind=kOutput, calls=%fused_computation.33 | convolution fusion | flops 1143341056 | bytes 10293248 | tf_op jit(solution)/shard_map/hck,kd->hcd/dot_general | solution.py:121
  105.4 2.7 convolution_convert_fusion
  108.2 149.9 %all-gather.6.cloned.1.call-done = bf16[2048,4096]{1,0:T(8,128)(2,1)} async-done(((bf16[256,4096]{1,0:T(8,128)(2,1)}), bf16[2048,4096]{1,0:T(8,128)(2,1)}) %all-gather.6.cloned.1.call-update) | async-done | bytes 16777232 | tf_op jit(solution)/shard_map/all_gather | solution.py:131
  258.1 10.5 %reduce_sum.41 = bf16[256,4096]{1,0:T(8,128)(2,1)} reduce(bf16[8,256,4096]{2,1,0:T(8,128)(2,1)} %bitcast.64, bf16[]{:T(256)} %constant.67.clone.1), dimensions={0}, to_apply=%region_3.4 | reduce | flops 7340032 | bytes 18874370 | tf_op jit(solution)/shard_map/reduce_sum | solution.py:130
  268.6 2.5 fusion.11
  271.1 1.3 copy-done.5
  272.4 6.3 %fusion.35 = f32[256,1376]{0,1:T(8,128)S(1)} fusion(bf16[4096,1376]{0,1:T(8,128)(2,1)} %param.20, bf16[256,4096]{1,0:T(8,128)(2,1)S(1)} %get-tuple-element.3, f32[4096]{0:T(1024)S(1)} %convert_element_type.89, f32[256]{0:T(256)S(1)} %add_rsqrt_fusion), kind=kOutput, calls=%fused_computation.42 | convolution fusion | flops 2889875456 | bytes 14795776 | tf_op jit(solution)/shard_map/dot_general | solution.py:139
  278.8 21.7 %fusion.10 = bf16[4096,256]{0,1:T(8,128)(2,1)} fusion(bf16[1376,4096]{1,0:T(8,128)(2,1)} %param.22, bf16[4096,1376]{0,1:T(8,128)(2,1)} %param.21, f32[256,1376]{0,1:T(8,128)S(1)} %fusion.35, bf16[256,4096]{1,0:T(8,128)(2,1)} %copy-done.5, f32[4096]{0:T(1024)S(1)} %convert_element_type.89, f32[256]{0:T(256)S(1)} %add_rsqrt_fusion), kind=kOutput, calls=%fused_computation.19 | convolution fusion | flops 5778718720 | bytes 28165120 | tf_op jit(solution)/shard_map/dot_general | solution.py:36
  301.5 33.3 %reduce-scatter.2.cloned.1.call-done = bf16[512,256]{0,1:T(8,128)(2,1)} async-done(((bf16[4096,256]{0,1:T(8,128)(2,1)}), bf16[512,256]{0,1:T(8,128)(2,1)}) %reduce-scatter.2.cloned.1.call-update) | async-done | bytes 262160 | tf_op jit(solution)/shard_map/reduce_scatter | solution.py:142
  334.7 1.8 fusion.41
  (60 shorter events, 8.5 us)
Async XLA Ops:
  7.2 39.2 %copy-start = (bf16[4096,128]{1,0:T(8,128)(2,1)S(1)}, bf16[4096,128]{1,0:T(8,128)(2,1)}, u32[]{:S(2)}) copy-start(bf16[4096,128]{1,0:T(8,128)(2,1)} %param.18) | copy-start | bytes 3145732
  7.2 36.9 %all-gather.4.cloned.1.call-start = ((), (), s32[]{:S(2)}) async-start(), calls=%async_computation.1 | async-start | bytes 2359296 | tf_op jit(solution)/shard_map/all_gather | solution.py:87
  7.9 250.1 %all-gather.6.cloned.1.call-start = ((), (), s32[]{:S(2)}) async-start(), calls=%async_computation.3 | async-start | bytes 18874368 | tf_op jit(solution)/shard_map/all_gather | solution.py:131
  8.6 15.9 %collective-permute-start.2 = (s32[2,8]{1,0:T(2,128)S(1)}, s32[2,8]{1,0:T(2,128)S(1)}, u32[]{:S(2)}, u32[]{:S(2)}) collective-permute-start(s32[2,8]{1,0:T(2,128)S(1)} %pad_add_fusion.1), channel_id=1, source_target_pairs={{0,24},{8,0},{16,8},{24,16},{1,25},{9,1},{17,9},{25,17},{2,26},{10... | collective-permute-start | bytes 200 | tf_op jit(solution)/shard_map/ppermute | solution.py:45
  12.5 12.0 %collective-permute-start.1 = (s32[2,8]{1,0:T(2,128)S(1)}, s32[2,8]{1,0:T(2,128)S(1)}, u32[]{:S(2)}, u32[]{:S(2)}) collective-permute-start(s32[2,8]{1,0:T(2,128)S(1)} %pad_add_fusion.1), channel_id=1, source_target_pairs={{0,16},{8,24},{16,0},{24,8},{1,17},{9,25},{17,1},{25,9},{2,18},{10... | collective-permute-start | bytes 200 | tf_op jit(solution)/shard_map/ppermute | solution.py:45
  13.0 11.5 %collective-permute-start = (s32[2,8]{1,0:T(2,128)S(1)}, s32[2,8]{1,0:T(2,128)S(1)}, u32[]{:S(2)}, u32[]{:S(2)}) collective-permute-start(s32[2,8]{1,0:T(2,128)S(1)} %pad_add_fusion.1), channel_id=1, source_target_pairs={{0,8},{8,16},{16,24},{24,0},{1,9},{9,17},{17,25},{25,1},{2,10},{10... | collective-permute-start | bytes 200 | tf_op jit(solution)/shard_map/ppermute | solution.py:45
  14.8 16.4 %collective-permute-start.5 = (bf16[8,128,256]{2,1,0:T(8,128)(2,1)S(1)}, bf16[8,128,256]{2,1,0:T(8,128)(2,1)S(1)}, u32[]{:S(2)}, u32[]{:S(2)}) collective-permute-start(bf16[8,128,256]{2,1,0:T(8,128)(2,1)S(1)} %pad_maximum_fusion.1), channel_id=1, source_target_pairs={{0,24},{8,0},{16,8},{24,16},{1,25},{9,1},{17,9},{25,17},{2,26},{10... | collective-permute-start | bytes 1572872 | tf_op jit(solution)/shard_map/ppermute | solution.py:45
  17.2 23.8 %collective-permute-start.4 = (bf16[8,128,256]{2,1,0:T(8,128)(2,1)S(1)}, bf16[8,128,256]{2,1,0:T(8,128)(2,1)S(1)}, u32[]{:S(2)}, u32[]{:S(2)}) collective-permute-start(bf16[8,128,256]{2,1,0:T(8,128)(2,1)S(1)} %pad_maximum_fusion.1), channel_id=1, source_target_pairs={{0,16},{8,24},{16,0},{24,8},{1,17},{9,25},{17,1},{25,9},{2,18},{10... | collective-permute-start | bytes 1572872 | tf_op jit(solution)/shard_map/ppermute | solution.py:45
  24.5 16.4 %collective-permute-start.3 = (bf16[8,128,256]{2,1,0:T(8,128)(2,1)S(1)}, bf16[8,128,256]{2,1,0:T(8,128)(2,1)S(1)}, u32[]{:S(2)}, u32[]{:S(2)}) collective-permute-start(bf16[8,128,256]{2,1,0:T(8,128)(2,1)S(1)} %pad_maximum_fusion.1), channel_id=1, source_target_pairs={{0,8},{8,16},{16,24},{24,0},{1,9},{9,17},{17,25},{25,1},{2,10},{10... | collective-permute-start | bytes 1572872 | tf_op jit(solution)/shard_map/ppermute | solution.py:45
  44.1 20.6 %copy-start.2 = (bf16[256,4096]{1,0:T(8,128)(2,1)S(1)}, bf16[256,4096]{1,0:T(8,128)(2,1)}, u32[]{:S(2)}) copy-start(bf16[256,4096]{1,0:T(8,128)(2,1)} %all-gather.4.cloned.1.call-done) | copy-start | bytes 6291460
  69.6 3.0 copy-start.4
  71.3 9.9 %copy-start.6 = (bf16[256,4,64]{2,0,1:T(8,128)(2,1)}, bf16[256,4,64]{2,0,1:T(8,128)(2,1)S(1)}, u32[]{:S(2)}) copy-start(bf16[256,4,64]{2,0,1:T(8,128)(2,1)S(1)} %get-tuple-element.11) | copy-start | bytes 393220
  81.3 18.8 %copy-start.9 = (bf16[256,128]{0,1:T(8,128)(2,1)S(1)}, bf16[256,128]{0,1:T(8,128)(2,1)}, u32[]{:S(2)}) copy-start(bf16[256,128]{0,1:T(8,128)(2,1)} %copy.21) | copy-start | bytes 196612
  100.1 5.3 %copy-start.3 = (bf16[512,4096]{1,0:T(8,128)(2,1)S(1)}, bf16[512,4096]{1,0:T(8,128)(2,1)}, u32[]{:S(2)}) copy-start(bf16[512,4096]{1,0:T(8,128)(2,1)} %param.19) | copy-start | bytes 12582916
  105.4 2.7 copy-start.10
  108.1 226.7 %reduce-scatter.2.cloned.1.call-start = ((), (), s32[]{:S(2)}) async-start(), calls=%async_computation.2 | async-start | bytes 2359296 | tf_op jit(solution)/shard_map/reduce_scatter | solution.py:142
  271.1 1.3 copy-start.5
  278.8 21.8 %copy-start.7 = (bf16[256,4,64]{2,0,1:T(8,128)(2,1)S(1)}, bf16[256,4,64]{2,0,1:T(8,128)(2,1)}, u32[]{:S(2)}) copy-start(bf16[256,4,64]{2,0,1:T(8,128)(2,1)} %copy-done.6) | copy-start | bytes 393220
  278.8 21.9 %copy-start.8 = (bf16[256,512]{1,0:T(8,128)(2,1)S(1)}, bf16[256,512]{1,0:T(8,128)(2,1)}, u32[]{:S(2)}) copy-start(bf16[256,512]{1,0:T(8,128)(2,1)} %get-tuple-element.12) | copy-start | bytes 786436
  278.8 57.8 %copy-start.1 = (bf16[4096,128]{1,0:T(8,128)(2,1)S(1)}, bf16[4096,128]{1,0:T(8,128)(2,1)}, u32[]{:S(2)}) copy-start(bf16[4096,128]{1,0:T(8,128)(2,1)} %param.18) | copy-start | bytes 3145732
Sparse Core Ops, SparseCore 0:
  9.6 31.7 all-gather.3
  108.2 149.8 all-gather.5
  300.7 33.9 reduce-scatter.1
